TPU v7x, 256 devices: a whole 4x4x8 slice. The times are simulated.
256 devices in a mesh: dp: 32 (over x, z), mp: 8 (over y, core).
Axes of the slice: x: 4, y: 4, z: 8, core: 2. Of those that a mesh axis runs over, the one named last changes fastest.
Arguments:
- tokens: bfloat16 [8192, 8192], P(('dp', 'mp')), may hold values from -6 to 6
- upstream: bfloat16 [8192, 2, 28672], P(('dp', 'mp')), may hold values from -0.0625 to 0.0625
- deltas: bfloat16 [1024, 128, 128], P('mp'), may hold values from -0.5 to 0.5
- block_row: int32 [1024], P('mp'), may hold values from 0 to 63, as said below
- block_column: int32 [1024], P('mp'), may hold values from 0 to 55, as said below
- block_owner: int32 [1024], P('mp'), may hold values from 0 to 31, as said below
- block_count: int32 [8], P('mp'), may hold values from 64 to 128, as said below
Outputs:
- branch_out: bfloat16 [8192, 2, 28672], P('dp', None, 'mp')
- block_grads: float32 [8, 192, 128, 128], P('mp', 'dp')
Inputs may be any that keep to these rules, and one draw needn't show every extreme that they name: `block_row`: row tile of each slot's delta tile. `block_column`: column tile within the shard's gate columns (below 28) followed by its up columns; the tiles of one shard's slots are distinct. `block_owner`: among the live slots of one shard no dp index owns more than 6 tiles, and in every shard one dp index owns exactly 6. The live slots of a shard are its first block_count slots; some shard has all 128 live.
All inputs are finite; a program needn't handle non-finite values.
Results may differ from a plain program's by a relative error of at most 0.001.
Values may be sent and summed in bfloat16 or wider, within the bound.
No kernel may reach another device: no remote copies, remote signals or barrier semaphores. Data moves between devices by JAX's collectives and lax.ppermute only.
A program may use at most 128 MiB of HBM per device.

v0:
```python
import jax
import jax.numpy as jnp
from jax import lax
from jax.sharding import PartitionSpec as P


def pick_tiles(source, chosen):
    slot_ids = jnp.arange(chosen.shape[1], dtype=jnp.int32)
    source_index = jnp.sum(jnp.where(chosen, slot_ids[None, :], 0), axis=1)
    present = jnp.any(chosen, axis=1).astype(jnp.float32)
    return jnp.take(source, source_index, axis=0) * present[:, None, None]


def local(tokens, upstream, deltas, block_row, block_column, block_owner, block_count):
    model_width = tokens.shape[1]
    tile_size = deltas.shape[1]
    slot_count = deltas.shape[0]
    hidden = lax.all_to_all(upstream, "mp", split_axis=2, concat_axis=0, tiled=True)
    group_rows = hidden.shape[0]
    column_blocks = hidden.shape[1] * hidden.shape[2] // tile_size
    hidden_major = jnp.transpose(hidden.reshape(group_rows, column_blocks, tile_size), (1, 0, 2))
    upstream_chosen = jnp.take(hidden_major, block_column, axis=0)
    slot_ids = jnp.arange(slot_count, dtype=jnp.int32)
    live_slots = slot_ids < block_count[0]
    column_table = (
        live_slots[:, None]
        & (block_column[:, None] == jnp.arange(column_blocks, dtype=jnp.int32)[None, :])
    ).astype(jnp.float32)
    shard_rows = lax.all_gather(tokens, "mp", axis=0, tiled=True)
    row_count = shard_rows.shape[0]
    row_major = jnp.transpose(
        shard_rows.reshape(row_count, model_width // tile_size, tile_size), (1, 0, 2)
    )
    feature_tiles = jnp.take(row_major, block_row, axis=0)
    product = jnp.einsum("kni,kio->kno", feature_tiles, deltas, preferred_element_type=jnp.float32)
    rows_out = jnp.einsum("kc,kno->cno", column_table, product, precision=lax.Precision.HIGHEST)
    placed = rows_out
    grad_sum = jnp.einsum(
        "kni,kno->kio", feature_tiles, upstream_chosen, preferred_element_type=jnp.float32
    )
    placed, grad_sum = (placed, grad_sum)
    branch_out = jnp.transpose(placed.astype(jnp.bfloat16), (1, 0, 2)).reshape(
        group_rows, hidden.shape[1], hidden.shape[2]
    )
    dp_count = lax.axis_size("dp")
    owner_cap = 3 * slot_count // (2 * dp_count)
    owner_hot = (
        (block_owner[:, None] == jnp.arange(dp_count, dtype=jnp.int32)[None, :])
        & live_slots[:, None]
    ).astype(jnp.int32)
    before = jnp.cumsum(owner_hot, axis=0) - owner_hot
    owner_rank = jnp.sum(before * owner_hot, axis=1)
    summed = lax.psum(grad_sum, "dp")
    my_owner = lax.axis_index("dp")
    chosen = (
        live_slots[None, :]
        & (block_owner[None, :] == my_owner)
        & (owner_rank[None, :] == jnp.arange(owner_cap, dtype=jnp.int32)[:, None])
    )
    owned = pick_tiles(summed, chosen)
    return (branch_out, owned[None])


def solution(mesh):
    placed = (
        P(("dp", "mp"), None),
        P(("dp", "mp"), None, None),
        P("mp", None, None),
        P("mp"),
        P("mp"),
        P("mp"),
        P("mp"),
    )
    return jax.shard_map(
        local,
        mesh=mesh,
        in_specs=placed,
        out_specs=(P("dp", None, "mp"), P("mp", "dp", None, None)),
        check_vma=False,
    )
```

profile of v0, /device:TPU:1, one launch (start us, length us, event | category | flops | bytes accessed | tf_op | source)
XLA Modules:
  0.0 435.7 jit_solution(1149873122995598057)
XLA Ops:
  7.2 0.0 all-gather.2.cloned.1.call-start
  7.2 0.7 all-gather.2.cloned.1.call-update
  7.9 34.9 %copy.36 = bf16[32,2,28672]{0,1,2:T(2,128)(2,1)} copy(bf16[32,2,28672]{2,1,0:T(2,128)(2,1)} %param.8) | data formatting | bytes 7340032 | tf_op args[1]
  42.8 0.0 copy-start.2
  42.8 16.5 %reshape.95 = bf16[8,2,114688]{2,1,0:T(2,128)(2,1)} reshape(bf16[28672,2,32]{2,1,0:T(2,128)(2,1)} %bitcast.26) | data formatting | bytes 7340032
  59.4 7.6 %all-to-all-start = ((bf16[8,2,114688]{2,1,0:T(2,128)(2,1)}), bf16[8,2,114688]{2,1,0:T(2,128)(2,1)}, u32[]{:S(2)}, u32[]{:S(2)}) async-start(bf16[8,2,114688]{2,1,0:T(2,128)(2,1)} %reshape.95), calls=%async_computation | async-start | bytes 7340032 | tf_op jit(solution)/shard_map/all_to_all | solution.py:18
  66.9 0.0 all-reduce.2.cloned.1.call-start
  66.9 0.0 copy-done.2
  67.0 0.0 copy-done.1
  67.0 43.1 %all-to-all-done = bf16[8,2,114688]{2,1,0:T(2,128)(2,1)} async-done(((bf16[8,2,114688]{2,1,0:T(2,128)(2,1)}), bf16[8,2,114688]{2,1,0:T(2,128)(2,1)}, u32[]{:S(2)}, u32[]{:S(2)}) %all-to-all-start) | async-done | bytes 3670048 | tf_op jit(solution)/shard_map/all_to_all | solution.py:18
  110.1 11.6 %reshape.96 = bf16[28672,2,32]{2,1,0:T(2,128)(2,1)} reshape(bf16[8,2,114688]{2,1,0:T(2,128)(2,1)} %all-to-all-done) | data formatting | bytes 7340032
  121.7 35.0 %copy.37 = bf16[32,2,8,3584]{3,1,0,2:T(2,128)(2,1)} copy(bf16[32,2,8,3584]{0,1,3,2:T(2,128)(2,1)} %bitcast.25) | data formatting | bytes 7340032 | tf_op jit(solution)/shard_map/all_to_all | solution.py:18
  156.8 9.2 %reshape.67 = bf16[256,56,128]{2,1,0:T(8,128)(2,1)} reshape(bf16[8,32,2,3584]{3,2,1,0:T(2,128)(2,1)} %bitcast.30) | data formatting | bytes 7340032 | tf_op jit(solution)/shard_map/reshape | solution.py:21
  165.9 4.8 %copy.46 = bf16[256,56,128]{2,0,1:T(8,128)(2,1)} copy(bf16[256,56,128]{2,1,0:T(8,128)(2,1)} %reshape.67) | data formatting | bytes 7340032 | tf_op jit(solution)/shard_map/reshape | solution.py:21
  170.7 8.6 %gather_fusion.1 = bf16[128,256,128]{2,1,0:T(8,128)(2,1)} fusion(bf16[56,256,128]{2,1,0:T(8,128)(2,1)} %bitcast.27, s32[1024]{0:T(1024)S(1)} %pad_clamp_fusion.1), kind=kCustom, calls=%fused_computation.1 | custom fusion | bytes 16777728 | tf_op jit(solution)/shard_map/jit(_take)/gather | solution.py:22
  179.3 6.4 %copy.33 = bf16[256,8192]{0,1:T(8,128)(2,1)} copy(bf16[256,8192]{1,0:T(8,128)(2,1)} %all-gather.2.cloned.1.call-done) | data formatting | bytes 8388608 | tf_op jit(solution)/shard_map/all_gather | solution.py:29
  185.7 6.4 %copy.34 = bf16[256,64,128]{2,0,1:T(8,128)(2,1)} copy(bf16[256,64,128]{0,2,1:T(8,128)(2,1)} %bitcast.29) | data formatting | bytes 8388608 | tf_op jit(solution)/shard_map/reshape | solution.py:32
  192.1 8.7 %gather_fusion = bf16[128,256,128]{2,1,0:T(8,128)(2,1)} fusion(bf16[64,256,128]{2,1,0:T(8,128)(2,1)} %bitcast.28, s32[1024]{0:T(1024)S(1)} %pad_clamp_fusion.2), kind=kCustom, calls=%fused_computation | custom fusion | bytes 16777728 | tf_op jit(solution)/shard_map/jit(_take)/gather | solution.py:34
  200.8 11.9 %fusion.2 = f32[128,128,128]{2,1,0:T(8,128)} fusion(bf16[128,256,128]{2,1,0:T(8,128)(2,1)} %gather_fusion.1, pred[128]{0:T(512)(128)(4,1)S(1)} %get-tuple-element.4, bf16[128,256,128]{2,1,0:T(8,128)(2,1)} %gather_fusion, pred[128]{0:T(512)(128)(4,1)S(1)} %get-tuple-element.5), kind=kOutput, calls=%fused_computation.5 | convolution fusion | flops 1082130432 | bytes 25166080 | tf_op jit(solution)/shard_map/kni,kno->kio/dot_general | solution.py:38
  212.7 0.0 all-reduce.2.cloned.1.call-update
  213.4 0.0 copy-done
  213.4 0.1 fusion.11
  213.5 0.2 reduce_window_sum.11
  213.7 0.2 select_reduce_fusion
  213.9 0.1 fusion.18
  214.0 0.1 select_reduce_fusion.1
  214.2 13.5 %fusion.6 = f32[128,256,128]{2,1,0:T(8,128)} fusion(bf16[128,128,128]{2,1,0:T(8,128)(2,1)} %param.9, bf16[128,256,128]{2,1,0:T(8,128)(2,1)} %gather_fusion, pred[128]{0:T(512)(128)(4,1)S(1)} %get-tuple-element.5), kind=kOutput, calls=%fused_computation.12 | convolution fusion | flops 1077936128 | bytes 29360256 | tf_op jit(solution)/shard_map/kni,kio->kno/dot_general | solution.py:35
  227.7 22.6 %convert_bitcast_fusion = bf16[256,56,128]{2,1,0:T(8,128)(2,1)} fusion(f32[128,256,128]{2,1,0:T(8,128)} %fusion.6, s32[128]{0:T(128)S(1)} %copy-done.1, pred[128]{0:T(512)(128)(4,1)S(1)} %get-tuple-element.3), kind=kOutput, calls=%fused_computation.11 | convolution fusion | flops 2820421632 | bytes 20447872 | tf_op jit(solution)/shard_map/kc,kno->cno/dot_general | solution.py:36
  250.4 8.2 %reshape.66 = bf16[256,2,3584]{2,1,0:T(2,128)(2,1)} reshape(bf16[256,56,128]{2,1,0:T(8,128)(2,1)} %convert_bitcast_fusion) | data formatting | bytes 7340032 | tf_op jit(solution)/shard_map/reshape | solution.py:42
  258.5 165.6 %all-reduce.2.cloned.1.call-done = f32[128,128,128]{2,1,0:T(8,128)} async-done(((f32[128,128,128]{2,1,0:T(8,128)}), f32[128,128,128]{2,1,0:T(8,128)}) %all-reduce.2.cloned.1.call-update) | async-done | bytes 8388624 | tf_op jit(solution)/shard_map/psum | solution.py:53
  424.1 4.0 gather_fusion.2
  428.0 0.9 fusion.9
  (13 shorter events, 0.1 us)
Async XLA Ops:
  7.2 172.2 %all-gather.2.cloned.1.call-start = ((), (), s32[]{:S(2)}) async-start(), calls=%async_computation.1 | async-start | bytes 4718592 | tf_op jit(solution)/shard_map/all_gather | solution.py:29
  42.8 24.1 %copy-start.2 = (s32[128]{0:T(128)S(1)}, s32[128]{0:T(128)}, u32[]{:S(2)}) copy-start(s32[128]{0:T(128)} %param.10) | copy-start | bytes 1540
  42.8 24.1 %copy-start.1 = (s32[128]{0:T(128)S(1)}, s32[128]{0:T(128)}, u32[]{:S(2)}) copy-start(s32[128]{0:T(128)} %param.11) | copy-start | bytes 1540
  59.4 50.7 %all-to-all-start = ((bf16[8,2,114688]{2,1,0:T(2,128)(2,1)}), bf16[8,2,114688]{2,1,0:T(2,128)(2,1)}, u32[]{:S(2)}, u32[]{:S(2)}) async-start(bf16[8,2,114688]{2,1,0:T(2,128)(2,1)} %reshape.95), calls=%async_computation | async-start | bytes 7340032 | tf_op jit(solution)/shard_map/all_to_all | solution.py:18
  66.9 357.1 %all-reduce.2.cloned.1.call-start = ((), (), s32[]{:S(2)}) async-start(), calls=%async_computation.2 | async-start | bytes 16777216 | tf_op jit(solution)/shard_map/psum | solution.py:53
  212.7 0.7 copy-start
Sparse Core Ops, SparseCore 0:
  9.8 38.8 all-gather.1
  212.9 211.1 all-reduce.1
where the time goes:
time: 440 us; the launch traced here: 436 us
  waiting for transfers between devices  209 us (48%)
  local copies, waits for them, and re-layouts  154 us (35%)
  matrix products  48.1 us (11%)
  between operations  14.8 us (3%)
  starting transfers between devices  7.59 us (2%)
    psum x1, waiting for transfers between devices, local(): summed = lax.psum(grad_sum, 'dp')  166 us
    unnamed x9, local copies, waits for them, and re-layouts  63.1 us
    all_to_all x1, waiting for transfers between devices, local(): lax.all_to_all(upstream, 'mp', split_axis=2, concat_axis=0, tiled=True)  43.1 us
    all_to_all x1, local copies, waits for them, and re-layouts, local(): lax.all_to_all(upstream, 'mp', split_axis=2, concat_axis=0, tiled=True)  35 us
    dot_general x1, matrix products, local(): jnp.einsum('kc,kno->cno', column_table, product, precision=lax.Precision....  22.6 us
    reshape x2, local copies, waits for them, and re-layouts, local(): hidden.reshape(group_rows, column_blocks, tile_size)  14 us
    dot_general x1, matrix products, local(): jnp.einsum('kni,kio->kno', feature_tiles, deltas, preferred_element_type=...  13.5 us
    dot_general x1, matrix products, local(): jnp.einsum('kni,kno->kio', feature_tiles, upstream_chosen, preferred_elem...  11.9 us
  transfers between devices with their start and end apart: 3, of which 2 were waited for; matrix products, arithmetic and copies ran while one was open for 38% of the time, Pallas kernels for 0%

commit v1 on v0

--- a/solution.py
+++ b/solution.py
@@ -1,7 +1,19 @@
+import functools
 import jax
 import jax.numpy as jnp
 from jax import lax
 from jax.sharding import PartitionSpec as P
+
+
+def marks_supply_all(state, device_axis):
+    earlier = lax.axis_size(device_axis)
+    out_arr = jnp.split(state, earlier, 2)
+    v_next = jnp.stack(out_arr, 0)
+    tmp = lax.all_to_all(v_next, device_axis, split_axis=0, concat_axis=0)
+    return jnp.concatenate(tmp, 0)
+
+
+_keep_up_tokens = functools.partial(marks_supply_all, device_axis="mp")
 
 
 def pick_tiles(source, chosen):
@@ -15,7 +27,7 @@
     model_width = tokens.shape[1]
     tile_size = deltas.shape[1]
     slot_count = deltas.shape[0]
-    hidden = lax.all_to_all(upstream, "mp", split_axis=2, concat_axis=0, tiled=True)
+    hidden = _keep_up_tokens(upstream)
     group_rows = hidden.shape[0]
     column_blocks = hidden.shape[1] * hidden.shape[2] // tile_size
     hidden_major = jnp.transpose(hidden.reshape(group_rows, column_blocks, tile_size), (1, 0, 2))

time: 440 us -> 367 us (0.83)
  local copies, waits for them, and re-layouts: 154 us -> 72.9 us
  waiting for transfers between devices: 209 us -> 220 us
    unnamed x9 -> x13, local copies, waits for them, and re-layouts: 63.1 us -> 14.7 us
    all_to_all x1 -> x0, local copies, waits for them, and re-layouts: 35 us -> none  [local(): lax.all_to_all(upstream, 'mp', split_axis=2, concat_axis=0, tiled=True)]
    another operation x0 -> x3, local copies, waits for them, and re-layouts: none -> 16.1 us  [the longest x2 13.9 us: local(): hidden.reshape(group_rows, column_blocks, tile_size)]
    reshape x2 -> x0, local copies, waits for them, and re-layouts: 14 us -> none  [local(): hidden.reshape(group_rows, column_blocks, tile_size)]
    all_to_all x1, waiting for transfers between devices: 43.1 us -> 54.1 us  [marks_supply_all(): tmp = lax.all_to_all(v_next, device_axis, split_axis=0, concat_axis=0)]
  transfers between devices with their start and end apart: 3 -> 3, of which waited for: 2 -> 2; matrix products, arithmetic and copies ran while one was open for 38% -> 23% of each run, Pallas kernels for 0% -> 0%
where the time goes in v1:
time: 367 us; the launch traced here: 365 us
  waiting for transfers between devices  220 us (60%)
  local copies, waits for them, and re-layouts  72.9 us (20%)
  matrix products  48.1 us (13%)
  between operations  14.8 us (4%)
  starting transfers between devices  7.65 us (2%)
    psum x1, waiting for transfers between devices, local(): summed = lax.psum(grad_sum, 'dp')  166 us
    all_to_all x1, waiting for transfers between devices, marks_supply_all(): tmp = lax.all_to_all(v_next, device_axis, split_axis=0, concat_axis=0)  54.1 us
    dot_general x1, matrix products, local(): jnp.einsum('kc,kno->cno', column_table, product, precision=lax.Precision....  22.6 us
    unnamed x13, local copies, waits for them, and re-layouts  14.7 us
    another operation x2, local copies, waits for them, and re-layouts, local(): hidden.reshape(group_rows, column_blocks, tile_size)  13.9 us
    dot_general x1, matrix products, local(): jnp.einsum('kni,kio->kno', feature_tiles, deltas, preferred_element_type=...  13.6 us
    dot_general x1, matrix products, local(): jnp.einsum('kni,kno->kio', feature_tiles, upstream_chosen, preferred_elem...  11.9 us
    gather x1, local copies, waits for them, and re-layouts, local(): feature_tiles = jnp.take(row_major, block_row, axis=0)  8.73 us
  transfers between devices with their start and end apart: 3, of which 2 were waited for; matrix products, arithmetic and copies ran while one was open for 23% of the time, Pallas kernels for 0%

profile of v1, /device:TPU:1, one launch (start us, length us, event | category | flops | bytes accessed | tf_op | source)
XLA Modules:
  0.0 365.4 jit_solution(15571713147260563371)
XLA Ops:
  7.2 0.0 all-gather.2.cloned.1.call-start
  7.2 0.7 all-gather.2.cloned.1.call-update
  7.9 2.1 bitcast_dynamic-update-slice_fusion.7
  10.0 2.1 bitcast_dynamic-update-slice_fusion.6
  12.1 2.1 bitcast_dynamic-update-slice_fusion.5
  14.2 2.1 bitcast_dynamic-update-slice_fusion.4
  16.3 2.1 bitcast_dynamic-update-slice_fusion.3
  18.4 2.1 bitcast_dynamic-update-slice_fusion.2
  20.5 2.1 bitcast_dynamic-update-slice_fusion.1
  22.6 2.1 bitcast_dynamic-update-slice_fusion
  24.7 7.6 %all-to-all-start = ((bf16[8,32,2,3584]{3,2,1,0:T(2,128)(2,1)}), bf16[8,32,2,3584]{3,2,1,0:T(2,128)(2,1)}, u32[]{:S(2)}, u32[]{:S(2)}) async-start(bf16[8,32,2,3584]{3,2,1,0:T(2,128)(2,1)} %bitcast_dynamic-update-slice_fusion), calls=%async_computation | async-start | bytes 7340032 | tf_op jit(solution)/shard_map/all_to_all | solution.py:12
  32.3 0.0 all-reduce.2.cloned.1.call-start
  32.4 54.1 %all-to-all-done = bf16[8,32,2,3584]{3,2,1,0:T(2,128)(2,1)} async-done(((bf16[8,32,2,3584]{3,2,1,0:T(2,128)(2,1)}), bf16[8,32,2,3584]{3,2,1,0:T(2,128)(2,1)}, u32[]{:S(2)}, u32[]{:S(2)}) %all-to-all-start) | async-done | bytes 3670048 | tf_op jit(solution)/shard_map/all_to_all | solution.py:12
  86.5 9.2 %reshape_reshape.3 = bf16[256,56,128]{2,1,0:T(8,128)(2,1)} reshape(bf16[8,32,2,3584]{3,2,1,0:T(2,128)(2,1)} %all-to-all-done) | data formatting | bytes 7340032 | tf_op jit(solution)/shard_map/reshape;reshape | solution.py:33
  95.7 4.8 %copy.32 = bf16[256,56,128]{2,0,1:T(8,128)(2,1)} copy(bf16[256,56,128]{2,1,0:T(8,128)(2,1)} %reshape_reshape.3) | data formatting | bytes 7340032 | tf_op jit(solution)/shard_map/reshape;reshape | solution.py:33
  100.4 8.6 %gather_fusion.1 = bf16[128,256,128]{2,1,0:T(8,128)(2,1)} fusion(bf16[56,256,128]{2,1,0:T(8,128)(2,1)} %bitcast.37, s32[1024]{0:T(1024)S(1)} %get-tuple-element.2), kind=kCustom, calls=%fused_computation.1 | custom fusion | bytes 16777728 | tf_op jit(solution)/shard_map/jit(_take)/gather | solution.py:34
  109.0 6.4 %copy.21 = bf16[256,8192]{0,1:T(8,128)(2,1)} copy(bf16[256,8192]{1,0:T(8,128)(2,1)} %all-gather.2.cloned.1.call-done) | data formatting | bytes 8388608 | tf_op jit(solution)/shard_map/all_gather | solution.py:41
  115.4 6.3 %copy.22 = bf16[256,64,128]{2,0,1:T(8,128)(2,1)} copy(bf16[256,64,128]{0,2,1:T(8,128)(2,1)} %bitcast.39) | data formatting | bytes 8388608 | tf_op jit(solution)/shard_map/reshape | solution.py:44
  121.7 8.7 %gather_fusion = bf16[128,256,128]{2,1,0:T(8,128)(2,1)} fusion(bf16[64,256,128]{2,1,0:T(8,128)(2,1)} %bitcast.38, s32[1024]{0:T(1024)S(1)} %get-tuple-element.3), kind=kCustom, calls=%fused_computation | custom fusion | bytes 16777728 | tf_op jit(solution)/shard_map/jit(_take)/gather | solution.py:46
  130.5 11.9 %fusion.2 = f32[128,128,128]{2,1,0:T(8,128)} fusion(bf16[128,256,128]{2,1,0:T(8,128)(2,1)} %gather_fusion.1, pred[128]{0:T(512)(128)(4,1)S(1)} %get-tuple-element.6, bf16[128,256,128]{2,1,0:T(8,128)(2,1)} %gather_fusion, pred[128]{0:T(512)(128)(4,1)S(1)} %get-tuple-element.7), kind=kOutput, calls=%fused_computation.5 | convolution fusion | flops 1082130432 | bytes 25166080 | tf_op jit(solution)/shard_map/kni,kno->kio/dot_general | solution.py:50
  142.4 0.0 all-reduce.2.cloned.1.call-update
  143.1 0.1 fusion.11
  143.2 0.2 reduce_window_sum.11
  143.4 0.2 select_reduce_fusion
  143.6 0.1 fusion.18
  143.7 0.1 select_reduce_fusion.1
  143.9 13.6 %fusion.6 = f32[128,256,128]{2,1,0:T(8,128)} fusion(bf16[128,128,128]{2,1,0:T(8,128)(2,1)} %param.9, bf16[128,256,128]{2,1,0:T(8,128)(2,1)} %gather_fusion, pred[128]{0:T(512)(128)(4,1)S(1)} %get-tuple-element.7), kind=kOutput, calls=%fused_computation.12 | convolution fusion | flops 1077936128 | bytes 29360256 | tf_op jit(solution)/shard_map/kni,kio->kno/dot_general | solution.py:47
  157.4 22.6 %convert_bitcast_fusion = bf16[256,56,128]{2,1,0:T(8,128)(2,1)} fusion(f32[128,256,128]{2,1,0:T(8,128)} %fusion.6, s32[128]{0:T(128)S(1)} %copy-done.1, pred[128]{0:T(512)(128)(4,1)S(1)} %get-tuple-element.5), kind=kOutput, calls=%fused_computation.11 | convolution fusion | flops 2820421632 | bytes 20447872 | tf_op jit(solution)/shard_map/kc,kno->cno/dot_general | solution.py:48
  180.1 8.2 %reshape.62 = bf16[256,2,3584]{2,1,0:T(2,128)(2,1)} reshape(bf16[256,56,128]{2,1,0:T(8,128)(2,1)} %convert_bitcast_fusion) | data formatting | bytes 7340032 | tf_op jit(solution)/shard_map/reshape | solution.py:54
  188.2 165.5 %all-reduce.2.cloned.1.call-done = f32[128,128,128]{2,1,0:T(8,128)} async-done(((f32[128,128,128]{2,1,0:T(8,128)}), f32[128,128,128]{2,1,0:T(8,128)}) %all-reduce.2.cloned.1.call-update) | async-done | bytes 8388624 | tf_op jit(solution)/shard_map/psum | solution.py:65
  353.8 4.0 %gather_fusion.2 = f32[6,128,128]{2,1,0:T(8,128)S(1)} fusion(f32[128,128,128]{2,1,0:T(8,128)} %all-reduce.2.cloned.1.call-done, s32[1024]{0:T(1024)S(1)} %pad_clamp_fusion), kind=kCustom, calls=%fused_computation.2 | custom fusion | bytes 786456 | tf_op jit(solution)/shard_map/jit(_take)/gather | solution.py:23
  357.7 0.9 fusion.9
  (16 shorter events, 0.1 us)
Async XLA Ops:
  7.2 101.9 %all-gather.2.cloned.1.call-start = ((), (), s32[]{:S(2)}) async-start(), calls=%async_computation.1 | async-start | bytes 4718592 | tf_op jit(solution)/shard_map/all_gather | solution.py:41
  22.6 9.7 %copy-start.2 = (s32[128]{0:T(128)S(1)}, s32[128]{0:T(128)}, u32[]{:S(2)}) copy-start(s32[128]{0:T(128)} %param.10) | copy-start | bytes 1540
  22.6 9.8 %copy-start.1 = (s32[128]{0:T(128)S(1)}, s32[128]{0:T(128)}, u32[]{:S(2)}) copy-start(s32[128]{0:T(128)} %param.11) | copy-start | bytes 1540
  24.7 61.7 %all-to-all-start = ((bf16[8,32,2,3584]{3,2,1,0:T(2,128)(2,1)}), bf16[8,32,2,3584]{3,2,1,0:T(2,128)(2,1)}, u32[]{:S(2)}, u32[]{:S(2)}) async-start(bf16[8,32,2,3584]{3,2,1,0:T(2,128)(2,1)} %bitcast_dynamic-update-slice_fusion), calls=%async_computation | async-start | bytes 7340032 | tf_op jit(solution)/shard_map/all_to_all | solution.py:12
  32.3 321.4 %all-reduce.2.cloned.1.call-start = ((), (), s32[]{:S(2)}) async-start(), calls=%async_computation.2 | async-start | bytes 16777216 | tf_op jit(solution)/shard_map/psum | solution.py:65
  142.4 0.7 copy-start
Sparse Core Ops, SparseCore 0:
  9.8 54.3 all-gather.1
  142.6 211.1 all-reduce.1
